TPU v7x, 256 devices: a whole 4x4x8 slice. The times are simulated.
256 devices in a mesh: expert: 16 (over z, core), tensor: 16 (over y, x).
Axes of the slice: x: 4, y: 4, z: 8, core: 2. Of those that a mesh axis runs over, the one named last changes fastest.
Arguments:
- residual_in: bfloat16 [22528, 1024], P(('expert', 'tensor')), may hold values from -6 to 6
- attn_heads: bfloat16 [1024, 22528], P('tensor', 'expert'), may hold values from -6 to 6
- out_proj: bfloat16 [1024, 1024], P('tensor'), may hold values from -0.1875 to 0.1875
- gain_first: float32 [1024], replicated, may hold values from 0.25 to 1.75
- router_weight: float32 [1024, 16], replicated, may hold values from -0.046875 to 0.046875
- routes: int32 [22528, 2], P(('expert', 'tensor')), may hold values from 0 to 15, all different within a row; in each aligned block of 88 rows (0 to 87, 88 to 175, ...) at most 22 rows name the same one
- w_gate: bfloat16 [16, 2816, 1024], P('expert', 'tensor'), may hold values from -0.1875 to 0.1875
- w_upward: bfloat16 [16, 2816, 1024], P('expert', 'tensor'), may hold values from -0.1875 to 0.1875
- w_downward: bfloat16 [16, 2816, 1024], P('expert', 'tensor'), may hold values from -0.21875 to 0.21875
- gain_second: float32 [1024], replicated, may hold values from 0.25 to 1.75
Outputs:
- residual_out: bfloat16 [22528, 1024], P(('expert', 'tensor'))
- next_normed: bfloat16 [22528, 1024], P(('expert', 'tensor'))
Inputs may be any that keep to these rules, and one draw needn't show every extreme that they name: `routes`: each row names two different experts; among the rows of one device no expert is named more than 22 times, and some expert reaches 22.
All inputs are finite; a program needn't handle non-finite values.
Results may differ from a plain program's by a relative error of at most 0.012.
Values may be sent and summed in bfloat16 or wider, within the bound.
No kernel may reach another device: no remote copies, remote signals or barrier semaphores. Data moves between devices by JAX's collectives and lax.ppermute only.
A program may use at most 128 MiB of HBM per device.

v0:
```python
import jax
import jax.numpy as jnp
from jax import lax
from jax.sharding import PartitionSpec as P


def rms_scale(values, gain):
    wide = values.astype(jnp.float32)
    scale = lax.rsqrt(jnp.mean(wide * wide, axis=-1, keepdims=True) + 1e-06)
    return (wide * scale * gain).astype(jnp.bfloat16)


def expert_block(inputs, gate_rows, up_rows, down_rows):
    gate_part = lax.dot_general(
        inputs, gate_rows, (((1,), (1,)), ((), ())), preferred_element_type=jnp.float32
    )
    up_part = lax.dot_general(
        inputs, up_rows, (((1,), (1,)), ((), ())), preferred_element_type=jnp.float32
    )
    hid = (jax.nn.gelu(gate_part, approximate=True) * up_part).astype(jnp.bfloat16)
    return jnp.dot(hid, down_rows, preferred_element_type=jnp.float32)


def per_device(
    residual_in,
    attn_heads,
    out_proj,
    gain_first,
    router_weight,
    routes,
    w_gate,
    w_upward,
    w_downward,
    gain_second,
):
    row_count = residual_in.shape[0]
    width = residual_in.shape[1]
    n_expert = lax.axis_size("expert")
    capacity = 4 * row_count // n_expert
    block = attn_heads
    projected = lax.psum_scatter(
        lax.dot_general(
            block, out_proj, (((0,), (0,)), ((), ())), preferred_element_type=jnp.float32
        ),
        "tensor",
        scatter_dimension=0,
        tiled=True,
    )
    hidden_one = (residual_in.astype(jnp.float32) + projected).astype(jnp.bfloat16)
    normed = rms_scale(hidden_one, gain_first)
    logits = jnp.dot(normed.astype(jnp.float32), router_weight, precision=lax.Precision.HIGHEST)
    router_probs = jax.nn.softmax(logits, axis=-1)
    picked = jnp.take_along_axis(router_probs, routes, axis=1)
    gate_weights = picked / jnp.sum(picked, axis=1, keepdims=True)
    flat_ids = routes.reshape(-1)
    expert_iota = jnp.arange(n_expert, dtype=jnp.int32)
    onehot = (flat_ids[:, None] == expert_iota[None, :]).astype(jnp.int32)
    earlier = jnp.cumsum(onehot, axis=0) - onehot
    slot_index = jnp.sum(earlier * onehot, axis=1)
    target = flat_ids * capacity + slot_index
    slot_iota = jnp.arange(n_expert * capacity, dtype=jnp.int32)
    placing = (slot_iota[:, None] == target[None, :]).astype(jnp.bfloat16)
    repeated = jnp.repeat(normed, 2, axis=0)
    send_slots = jnp.dot(placing, repeated, preferred_element_type=jnp.float32).astype(jnp.bfloat16)
    send_slots = send_slots.reshape(n_expert, capacity, width)
    received = lax.all_to_all(send_slots, "expert", split_axis=0, concat_axis=0, tiled=True)
    slot_total = n_expert * capacity
    rows_in = received.reshape(slot_total, width)
    gate_rows = w_gate[0]
    up_rows = w_upward[0]
    down_rows = w_downward[0]
    all_rows = lax.all_gather(rows_in, "tensor", axis=0, tiled=True)
    block = all_rows
    expert_sum = lax.psum_scatter(
        expert_block(block, gate_rows, up_rows, down_rows).astype(jnp.bfloat16),
        "tensor",
        scatter_dimension=0,
        tiled=True,
    )
    expert_out = expert_sum.reshape(n_expert, capacity, width)
    returned = lax.all_to_all(expert_out, "expert", split_axis=0, concat_axis=0, tiled=True)
    returned = returned.reshape(slot_total, width)
    per_route = lax.dot_general(
        placing, returned, (((0,), (0,)), ((), ())), preferred_element_type=jnp.float32
    )
    per_route = per_route.reshape(row_count, 2, width)
    mixed = jnp.sum(gate_weights[:, :, None] * per_route, axis=1)
    residual_out = (hidden_one.astype(jnp.float32) + mixed).astype(jnp.bfloat16)
    next_normed = rms_scale(residual_out, gain_second)
    return (residual_out, next_normed)


def solution(mesh):
    placed = (
        P(("expert", "tensor"), None),
        P("tensor", "expert"),
        P("tensor", None),
        P(),
        P(),
        P(("expert", "tensor"), None),
        P("expert", "tensor", None),
        P("expert", "tensor", None),
        P("expert", "tensor", None),
        P(),
    )
    return jax.shard_map(
        per_device,
        mesh=mesh,
        in_specs=placed,
        out_specs=(P(("expert", "tensor"), None), P(("expert", "tensor"), None)),
        check_vma=False,
    )
```

profile of v0, /device:TPU:1, one launch (start us, length us, event | category | flops | bytes accessed | tf_op | source)
XLA Modules:
  0.0 380.7 jit_solution(14872669456772548435)
XLA Ops:
  7.2 4.4 %fusion.38 = f32[1408,1024]{1,0:T(8,128)} fusion(bf16[64,1408]{1,0:T(8,128)(2,1)} %param.11, bf16[64,1024]{1,0:T(8,128)(2,1)} %param.12), kind=kOutput, calls=%fused_computation.66 | convolution fusion | flops 184549376 | bytes 6078464 | tf_op jit(solution)/shard_map/dot_general | solution.py:42
  11.7 0.6 copy-done.5
  12.6 0.6 reduce-window.6
  13.2 0.2 slice_reduce_fusion
  13.5 86.2 %reduce-scatter.7.cloned.1.call-done = f32[88,1024]{1,0:T(8,128)} async-done(((f32[1408,1024]{1,0:T(8,128)}), f32[88,1024]{1,0:T(8,128)}) %reduce-scatter.7.cloned.1.call-update) | async-done | bytes 360464
  99.7 1.1 fusion.16
  101.0 0.2 broadcast_in_dim.7
  101.4 0.3 convolution_convert_fusion.1
  101.7 0.2 reshape.113
  101.9 32.1 %all_to_all.10 = bf16[16,22,1024]{2,1,0:T(8,128)(2,1)S(1)} all-to-all(bf16[16,22,1024]{2,1,0:T(8,128)(2,1)S(1)} %reshape.113), channel_id=1, replica_groups=mesh['expert'=16,'tensor'=16] {'expert'}, dimensions={0} | all-to-all | bytes 1441792 | tf_op jit(solution)/shard_map/all_to_all | solution.py:66
  134.1 1.1 reshape.114
  135.2 84.5 %all-gather.2.cloned.1.call-done = bf16[5632,1024]{1,0:T(8,128)(2,1)} async-done(((bf16[352,1024]{1,0:T(8,128)(2,1)}), bf16[5632,1024]{1,0:T(8,128)(2,1)}) %all-gather.2.cloned.1.call-update) | async-done | bytes 11534352 | tf_op jit(solution)/shard_map/all_gather | solution.py:72
  219.7 10.2 %fusion.23 = f32[5632,176]{0,1:T(8,128)} fusion(bf16[5632,1024]{1,0:T(8,128)(2,1)} %all-gather.2.cloned.1.call-done, bf16[1,176,1024]{2,1,0:T(8,128)(2,1)S(1)} %copy-done.2), kind=kOutput, calls=%fused_computation.33 | convolution fusion | flops 2030043136 | bytes 15859712 | tf_op jit(solution)/shard_map/dot_general | solution.py:14
  229.9 13.1 %convolution_convert_fusion = bf16[5632,1024]{1,0:T(8,128)(2,1)} fusion(bf16[5632,1024]{1,0:T(8,128)(2,1)} %all-gather.2.cloned.1.call-done, f32[5632,176]{0,1:T(8,128)} %fusion.23, bf16[1,176,1024]{2,1,0:T(8,128)(2,1)S(1)} %copy-done, bf16[1,176,1024]{2,1,0:T(8,128)(2,1)S(1)} %copy-done.8), kind=kOutput, calls=%fused_computation.1 | convolution fusion | flops 4075765760 | bytes 27754496 | tf_op jit(solution)/shard_map/dot_general | solution.py:21
  243.0 96.4 %reduce-scatter.5.cloned.1.call-done = bf16[352,1024]{1,0:T(8,128)(2,1)} async-done(((bf16[5632,1024]{1,0:T(8,128)(2,1)}), bf16[352,1024]{1,0:T(8,128)(2,1)}) %reduce-scatter.5.cloned.1.call-update) | async-done | bytes 720912 | tf_op jit(solution)/shard_map/reduce_scatter | solution.py:74
  339.5 2.1 reshape.115
  341.6 8.3 %all-to-all-start.1 = ((bf16[16,22,1024]{2,1,0:T(8,128)(2,1)}), bf16[16,22,1024]{2,1,0:T(8,128)(2,1)S(1)}, u32[]{:S(2)}, u32[]{:S(2)}) async-start(bf16[16,22,1024]{2,1,0:T(8,128)(2,1)} %reshape.115), calls=%async_computation.2 | async-start | bytes 1572864 | tf_op jit(solution)/shard_map/all_to_all | solution.py:81
  350.4 0.3 fusion.37
  350.7 2.3 gather_fusion
  353.2 19.4 %all-to-all-done.1 = bf16[16,22,1024]{2,1,0:T(8,128)(2,1)S(1)} async-done(((bf16[16,22,1024]{2,1,0:T(8,128)(2,1)}), bf16[16,22,1024]{2,1,0:T(8,128)(2,1)S(1)}, u32[]{:S(2)}, u32[]{:S(2)}) %all-to-all-start.1) | async-done | bytes 720928 | tf_op jit(solution)/shard_map/all_to_all | solution.py:81
  372.6 0.2 reshape.129
  372.8 0.4 fusion.12
  373.2 0.2 fusion.13
  373.4 0.8 fusion.15
  (47 shorter events, 1.6 us)
Async XLA Ops:
  7.2 222.7 %copy-start = (bf16[1,176,1024]{2,1,0:T(8,128)(2,1)S(1)}, bf16[1,176,1024]{2,1,0:T(8,128)(2,1)}, u32[]{:S(2)}) copy-start(bf16[1,176,1024]{2,1,0:T(8,128)(2,1)} %param.18) | copy-start | bytes 1081348
  7.2 92.5 %reduce-scatter.7.cloned.1.call-start = ((), (), s32[]{:S(2)}) async-start(), calls=%async_computation.6 | async-start | bytes 6127616
  11.7 0.7 copy-start.5
  11.7 88.1 %copy-start.3 = (bf16[88,1024]{1,0:T(8,128)(2,1)S(1)}, bf16[88,1024]{1,0:T(8,128)(2,1)}, u32[]{:S(2)}) copy-start(bf16[88,1024]{1,0:T(8,128)(2,1)} %param.10) | copy-start | bytes 540676
  11.7 89.2 %copy-start.6 = (f32[1024]{0:T(1024)S(1)}, f32[1024]{0:T(1024)}, u32[]{:S(2)}) copy-start(f32[1024]{0:T(1024)} %param.13) | copy-start | bytes 12292
  11.7 208.0 %all-gather.2.cloned.1.call-start = ((), (), s32[]{:S(2)}) async-start(), calls=%async_computation.4 | async-start | bytes 12255232 | tf_op jit(solution)/shard_map/all_gather | solution.py:72
  100.9 118.8 %copy-start.2 = (bf16[1,176,1024]{2,1,0:T(8,128)(2,1)S(1)}, bf16[1,176,1024]{2,1,0:T(8,128)(2,1)}, u32[]{:S(2)}) copy-start(bf16[1,176,1024]{2,1,0:T(8,128)(2,1)} %param.16) | copy-start | bytes 1081348
  135.1 94.8 %copy-start.8 = (bf16[1,176,1024]{2,1,0:T(8,128)(2,1)S(1)}, bf16[1,176,1024]{2,1,0:T(8,128)(2,1)}, u32[]{:S(2)}) copy-start(bf16[1,176,1024]{2,1,0:T(8,128)(2,1)} %param.17) | copy-start | bytes 1081348
  135.2 204.3 %reduce-scatter.5.cloned.1.call-start = ((), (), s32[]{:S(2)}) async-start(), calls=%async_computation.5 | async-start | bytes 12255232 | tf_op jit(solution)/shard_map/reduce_scatter | solution.py:74
  243.0 107.4 %copy-start.4 = (f32[1024,16]{0,1:T(8,128)S(1)}, f32[1024,16]{0,1:T(8,128)}, u32[]{:S(2)}) copy-start(f32[1024,16]{0,1:T(8,128)} %param.14) | copy-start | bytes 196612
  341.6 31.1 %all-to-all-start.1 = ((bf16[16,22,1024]{2,1,0:T(8,128)(2,1)}), bf16[16,22,1024]{2,1,0:T(8,128)(2,1)S(1)}, u32[]{:S(2)}, u32[]{:S(2)}) async-start(bf16[16,22,1024]{2,1,0:T(8,128)(2,1)} %reshape.115), calls=%async_computation.2 | async-start | bytes 1572864 | tf_op jit(solution)/shard_map/all_to_all | solution.py:81
  350.7 22.7 %copy-start.7 = (f32[1024]{0:T(1024)S(1)}, f32[1024]{0:T(1024)}, u32[]{:S(2)}) copy-start(f32[1024]{0:T(1024)} %param.19) | copy-start | bytes 12292
  373.3 0.8 copy-start.1
Sparse Core Ops, SparseCore 0:
  11.8 87.8 reduce-scatter.6
  135.3 84.3 all-gather.1
  243.2 96.2 reduce-scatter.4
where the time goes:
time: 381 us
  waiting for transfers between devices  287 us (75%)
  blocking collectives  32.1 us (8%)
  matrix products  28.7 us (8%)
  between operations  14 us (4%)
  starting transfers between devices  8.46 us (2%)
  local copies, waits for them, and re-layouts  7.73 us (2%)
    reduce_scatter x1, waiting for transfers between devices, per_device(): lax.psum_scatter(expert_block(block, gate_rows, up_rows, down_rows).astyp...  96.4 us
    unnamed x4, waiting for transfers between devices  86.2 us
    all_gather x1, waiting for transfers between devices, per_device(): all_rows = lax.all_gather(rows_in, 'tensor', axis=0, tiled=True)  84.5 us
    all_to_all x1, blocking collectives, per_device(): lax.all_to_all(send_slots, 'expert', split_axis=0, concat_axis=0, tiled=T...  32.1 us
    all_to_all x1, waiting for transfers between devices, per_device(): lax.all_to_all(expert_out, 'expert', split_axis=0, concat_axis=0, tiled=T...  19.4 us
    dot_general x1, matrix products, expert_block(): return jnp.dot(hid, down_rows, preferred_element_type=jnp.float32)  13.1 us
    dot_general x1, matrix products, expert_block(): lax.dot_general(inputs, gate_rows, (((1,), (1,)), ((), ())), preferred_el...  10.2 us
    all_to_all x1, starting transfers between devices, per_device(): lax.all_to_all(expert_out, 'expert', split_axis=0, concat_axis=0, tiled=T...  8.33 us
  transfers between devices with their start and end apart: 4, of which 4 were waited for; matrix products, arithmetic and copies ran while one was open for 1% of the time, Pallas kernels for 0%

commit v1 on v0

--- a/solution.py
+++ b/solution.py
@@ -2,6 +2,12 @@
 import jax.numpy as jnp
 from jax import lax
 from jax.sharding import PartitionSpec as P
+
+
+def in_order(tiles, dim):
+    tiles = jnp.moveaxis(tiles, 0, dim)
+    lengths = tiles.shape
+    return tiles.reshape(*lengths[:dim], lengths[dim] * lengths[dim + 1], *lengths[dim + 2 :])
 
 
 def rms_scale(values, gain):
@@ -69,7 +75,19 @@
     gate_rows = w_gate[0]
     up_rows = w_upward[0]
     down_rows = w_downward[0]
-    all_rows = lax.all_gather(rows_in, "tensor", axis=0, tiled=True)
+    peers = lax.axis_size("tensor")
+    pairs = [(i, (i + 1) % peers) for i in range(peers)]
+    back = [(b, a) for a, b in pairs]
+    lower, upper = ([], [])
+    for step in range(peers - 1):
+        if step % 2 == 0:
+            lower.append(lax.ppermute(lower[-1] if lower else rows_in, "tensor", pairs))
+        else:
+            upper.append(lax.ppermute(upper[-1] if upper else rows_in, "tensor", back))
+    blocks = jnp.stack([*lower[::-1], rows_in, *upper])
+    shift = lax.axis_index("tensor") - len(lower)
+    blocks = blocks[(jnp.arange(peers) - shift) % peers]
+    all_rows = in_order(blocks, 0)
     block = all_rows
     expert_sum = lax.psum_scatter(
         expert_block(block, gate_rows, up_rows, down_rows).astype(jnp.bfloat16),

time: 381 us -> 476 us (1.25)
  starting transfers between devices: 8.46 us -> 44 us
  local copies, waits for them, and re-layouts: 7.73 us -> 42.8 us
  waiting for transfers between devices: 287 us -> 310 us
    ppermute x0 -> x15, waiting for transfers between devices: none -> 111 us  [the longest x8 111 us: per_device(): lower.append(lax.ppermute(lower[-1] if lower else rows_in, 'tensor', pairs))]
    all_gather x1 -> x0, waiting for transfers between devices: 84.5 us -> none  [per_device(): all_rows = lax.all_gather(rows_in, 'tensor', axis=0, tiled=True)]
    ppermute x0 -> x15, starting transfers between devices: none -> 35.6 us  [the longest x7 34.6 us: per_device(): upper.append(lax.ppermute(upper[-1] if upper else rows_in, 'tensor', back))]
    unnamed x19 -> x62, local copies, waits for them, and re-layouts: 0.74 us -> 25.1 us
    gather x0 -> x1, local copies, waits for them, and re-layouts: none -> 10.4 us  [per_device(): blocks = blocks[(jnp.arange(peers) - shift) % peers]]
    unnamed x4 -> x3, waiting for transfers between devices: 86.2 us -> 86.6 us
  transfers between devices with their start and end apart: 4 -> 18, of which waited for: 4 -> 11; matrix products, arithmetic and copies ran while one was open for 1% -> 6% of each run, Pallas kernels for 0% -> 0%
where the time goes in v1:
time: 476 us
  waiting for transfers between devices  310 us (65%)
  starting transfers between devices  44 us (9%)
  local copies, waits for them, and re-layouts  42.8 us (9%)
  blocking collectives  32.1 us (7%)
  matrix products  28.9 us (6%)
  between operations  14.4 us (3%)
    ppermute x8, waiting for transfers between devices, per_device(): lower.append(lax.ppermute(lower[-1] if lower else rows_in, 'tensor', pairs))  111 us
    reduce_scatter x1, waiting for transfers between devices, per_device(): lax.psum_scatter(expert_block(block, gate_rows, up_rows, down_rows).astyp...  93.4 us
    unnamed x3, waiting for transfers between devices  86.6 us
    ppermute x7, starting transfers between devices, per_device(): upper.append(lax.ppermute(upper[-1] if upper else rows_in, 'tensor', back))  34.6 us
    all_to_all x1, blocking collectives, per_device(): lax.all_to_all(send_slots, 'expert', split_axis=0, concat_axis=0, tiled=T...  32.1 us
    unnamed x62, local copies, waits for them, and re-layouts  25.1 us
    all_to_all x1, waiting for transfers between devices, per_device(): lax.all_to_all(expert_out, 'expert', split_axis=0, concat_axis=0, tiled=T...  19.4 us
    dot_general x1, matrix products, expert_block(): return jnp.dot(hid, down_rows, preferred_element_type=jnp.float32)  13.1 us
  transfers between devices with their start and end apart: 18, of which 11 were waited for; matrix products, arithmetic and copies ran while one was open for 6% of the time, Pallas kernels for 0%

profile of v1, /device:TPU:1, one launch (start us, length us, event | category | flops | bytes accessed | tf_op | source)
XLA Modules:
  0.0 475.5 jit_solution(2142085877555331518)
XLA Ops:
  7.3 4.5 fusion.40
  13.1 86.5 %reduce-scatter.7.cloned.1.call-done = f32[88,1024]{1,0:T(8,128)} async-done(((f32[1408,1024]{1,0:T(8,128)}), f32[88,1024]{1,0:T(8,128)}) %reduce-scatter.7.cloned.1.call-update) | async-done | bytes 360464
  101.8 32.1 %all_to_all.10 = bf16[16,22,1024]{2,1,0:T(8,128)(2,1)S(1)} all-to-all(bf16[16,22,1024]{2,1,0:T(8,128)(2,1)S(1)} %reshape.165), channel_id=1, replica_groups=mesh['expert'=16,'tensor'=16] {'expert'}, dimensions={0} | all-to-all | bytes 1441792 | tf_op jit(solution)/shard_map/all_to_all | solution.py:72
  135.1 20.5 %collective-permute-done = bf16[352,1024]{1,0:T(8,128)(2,1)S(1)} collective-permute-done((bf16[352,1024]{1,0:T(8,128)(2,1)S(1)}, bf16[352,1024]{1,0:T(8,128)(2,1)S(1)}, u32[]{:S(2)}, u32[]{:S(2)}) %collective-permute-start) | collective-permute-done | bytes 720928 | tf_op jit(solution)/shard_map/ppermute | solution.py:84
  155.6 4.8 %collective-permute-start.8 = (bf16[352,1024]{1,0:T(8,128)(2,1)}, bf16[352,1024]{1,0:T(8,128)(2,1)S(1)}, u32[]{:S(2)}, u32[]{:S(2)}) collective-permute-start(bf16[352,1024]{1,0:T(8,128)(2,1)} %copy-done.14), channel_id=1, source_target_pairs={{1,0},{2,1},{3,2},{4,3},{5,4},{6,5},{7,6},{8,7},{9,8},{10,9},{11,1... | collective-permute-start | bytes 2162696 | tf_op jit(solution)/shard_map/ppermute | solution.py:86
  160.4 15.7 %collective-permute-done.1 = bf16[352,1024]{1,0:T(8,128)(2,1)S(1)} collective-permute-done((bf16[352,1024]{1,0:T(8,128)(2,1)S(1)}, bf16[352,1024]{1,0:T(8,128)(2,1)S(1)}, u32[]{:S(2)}, u32[]{:S(2)}) %collective-permute-start.1) | collective-permute-done | bytes 720928 | tf_op jit(solution)/shard_map/ppermute | solution.py:84
  176.2 4.8 %collective-permute-start.9 = (bf16[352,1024]{1,0:T(8,128)(2,1)S(1)}, bf16[352,1024]{1,0:T(8,128)(2,1)S(1)}, u32[]{:S(2)}, u32[]{:S(2)}) collective-permute-start(bf16[352,1024]{1,0:T(8,128)(2,1)S(1)} %collective-permute-done.8), channel_id=1, source_target_pairs={{1,0},{2,1},{3,2},{4,3},{5,4},{6,5},{7,6},{8,7},{9,8},{10,9},{11,1... | collective-permute-start | bytes 2162696 | tf_op jit(solution)/shard_map/ppermute | solution.py:86
  180.9 14.9 %collective-permute-done.2 = bf16[352,1024]{1,0:T(8,128)(2,1)S(1)} collective-permute-done((bf16[352,1024]{1,0:T(8,128)(2,1)S(1)}, bf16[352,1024]{1,0:T(8,128)(2,1)S(1)}, u32[]{:S(2)}, u32[]{:S(2)}) %collective-permute-start.2) | collective-permute-done | bytes 720928 | tf_op jit(solution)/shard_map/ppermute | solution.py:84
  195.8 4.8 %collective-permute-start.10 = (bf16[352,1024]{1,0:T(8,128)(2,1)S(1)}, bf16[352,1024]{1,0:T(8,128)(2,1)S(1)}, u32[]{:S(2)}, u32[]{:S(2)}) collective-permute-start(bf16[352,1024]{1,0:T(8,128)(2,1)S(1)} %collective-permute-done.9), channel_id=1, source_target_pairs={{1,0},{2,1},{3,2},{4,3},{5,4},{6,5},{7,6},{8,7},{9,8},{10,9},{11,1... | collective-permute-start | bytes 2162696 | tf_op jit(solution)/shard_map/ppermute | solution.py:86
  200.7 14.0 %collective-permute-done.3 = bf16[352,1024]{1,0:T(8,128)(2,1)S(1)} collective-permute-done((bf16[352,1024]{1,0:T(8,128)(2,1)S(1)}, bf16[352,1024]{1,0:T(8,128)(2,1)S(1)}, u32[]{:S(2)}, u32[]{:S(2)}) %collective-permute-start.3) | collective-permute-done | bytes 720928 | tf_op jit(solution)/shard_map/ppermute | solution.py:84
  214.7 4.8 %collective-permute-start.11 = (bf16[352,1024]{1,0:T(8,128)(2,1)S(1)}, bf16[352,1024]{1,0:T(8,128)(2,1)S(1)}, u32[]{:S(2)}, u32[]{:S(2)}) collective-permute-start(bf16[352,1024]{1,0:T(8,128)(2,1)S(1)} %collective-permute-done.10), channel_id=1, source_target_pairs={{1,0},{2,1},{3,2},{4,3},{5,4},{6,5},{7,6},{8,7},{9,8},{10,9},{11,1... | collective-permute-start | bytes 2162696 | tf_op jit(solution)/shard_map/ppermute | solution.py:86
  219.5 13.1 %collective-permute-done.4 = bf16[352,1024]{1,0:T(8,128)(2,1)S(1)} collective-permute-done((bf16[352,1024]{1,0:T(8,128)(2,1)S(1)}, bf16[352,1024]{1,0:T(8,128)(2,1)S(1)}, u32[]{:S(2)}, u32[]{:S(2)}) %collective-permute-start.4) | collective-permute-done | bytes 720928 | tf_op jit(solution)/shard_map/ppermute | solution.py:84
  233.6 4.7 collective-permute-start.12
  238.3 11.4 %collective-permute-done.5 = bf16[352,1024]{1,0:T(8,128)(2,1)S(1)} collective-permute-done((bf16[352,1024]{1,0:T(8,128)(2,1)S(1)}, bf16[352,1024]{1,0:T(8,128)(2,1)S(1)}, u32[]{:S(2)}, u32[]{:S(2)}) %collective-permute-start.5) | collective-permute-done | bytes 720928 | tf_op jit(solution)/shard_map/ppermute | solution.py:84
  249.7 5.5 %collective-permute-start.13 = (bf16[352,1024]{1,0:T(8,128)(2,1)}, bf16[352,1024]{1,0:T(8,128)(2,1)}, u32[]{:S(2)}, u32[]{:S(2)}) collective-permute-start(bf16[352,1024]{1,0:T(8,128)(2,1)} %collective-permute-done.12), channel_id=1, source_target_pairs={{1,0},{2,1},{3,2},{4,3},{5,4},{6,5},{7,6},{8,7},{9,8},{10,9},{11,1... | collective-permute-start | bytes 2162696 | tf_op jit(solution)/shard_map/ppermute | solution.py:86
  255.2 10.8 %collective-permute-done.6 = bf16[352,1024]{1,0:T(8,128)(2,1)} collective-permute-done((bf16[352,1024]{1,0:T(8,128)(2,1)S(1)}, bf16[352,1024]{1,0:T(8,128)(2,1)}, u32[]{:S(2)}, u32[]{:S(2)}) %collective-permute-start.6) | collective-permute-done | bytes 720928 | tf_op jit(solution)/shard_map/ppermute | solution.py:84
  266.4 5.1 %collective-permute-start.14 = (bf16[352,1024]{1,0:T(8,128)(2,1)}, bf16[352,1024]{1,0:T(8,128)(2,1)S(1)}, u32[]{:S(2)}, u32[]{:S(2)}) collective-permute-start(bf16[352,1024]{1,0:T(8,128)(2,1)} %collective-permute-done.13), channel_id=1, source_target_pairs={{1,0},{2,1},{3,2},{4,3},{5,4},{6,5},{7,6},{8,7},{9,8},{10,9},{11,1... | collective-permute-start | bytes 2162696 | tf_op jit(solution)/shard_map/ppermute | solution.py:86
  271.5 10.3 %collective-permute-done.7 = bf16[352,1024]{1,0:T(8,128)(2,1)} collective-permute-done((bf16[352,1024]{1,0:T(8,128)(2,1)}, bf16[352,1024]{1,0:T(8,128)(2,1)}, u32[]{:S(2)}, u32[]{:S(2)}) %collective-permute-start.7) | collective-permute-done | bytes 720928 | tf_op jit(solution)/shard_map/ppermute | solution.py:84
  306.7 10.4 %gather_fusion = bf16[16,352,1024]{2,1,0:T(8,128)(2,1)} fusion(bf16[16,352,1024]{2,1,0:T(8,128)(2,1)} %bitcast_dynamic-update-slice_fusion, s32[1024]{0:T(1024)S(1)} %pad_clamp_fusion), kind=kCustom, calls=%fused_computation | custom fusion | bytes 23068736 | tf_op jit(solution)/shard_map/gather | solution.py:89
  317.1 10.2 %fusion.23 = f32[5632,176]{0,1:T(8,128)} fusion(bf16[5632,1024]{1,0:T(8,128)(2,1)} %bitcast.68, bf16[1,176,1024]{2,1,0:T(8,128)(2,1)S(1)} %copy-done.16), kind=kOutput, calls=%fused_computation.49 | convolution fusion | flops 2030043136 | bytes 15859712 | tf_op jit(solution)/shard_map/dot_general | solution.py:20
  327.3 13.1 %convolution_convert_fusion = bf16[5632,1024]{1,0:T(8,128)(2,1)} fusion(bf16[5632,1024]{1,0:T(8,128)(2,1)} %bitcast.69, f32[5632,176]{0,1:T(8,128)} %fusion.23, bf16[1,176,1024]{2,1,0:T(8,128)(2,1)S(1)} %copy-done, bf16[1,176,1024]{2,1,0:T(8,128)(2,1)S(1)} %copy-done.22), kind=kOutput, calls=%fused_computation.2 | convolution fusion | flops 4075765760 | bytes 27754496 | tf_op jit(solution)/shard_map/dot_general | solution.py:27
  340.5 93.4 %reduce-scatter.5.cloned.1.call-done = bf16[352,1024]{1,0:T(8,128)(2,1)} async-done(((bf16[5632,1024]{1,0:T(8,128)(2,1)}), bf16[352,1024]{1,0:T(8,128)(2,1)}) %reduce-scatter.5.cloned.1.call-update) | async-done | bytes 720912 | tf_op jit(solution)/shard_map/reduce_scatter | solution.py:92
  436.1 8.4 %all-to-all-start.1 = ((bf16[16,22,1024]{2,1,0:T(8,128)(2,1)}), bf16[16,22,1024]{2,1,0:T(8,128)(2,1)S(1)}, u32[]{:S(2)}, u32[]{:S(2)}) async-start(bf16[16,22,1024]{2,1,0:T(8,128)(2,1)} %reshape.168), calls=%async_computation.2 | async-start | bytes 1572864 | tf_op jit(solution)/shard_map/all_to_all | solution.py:99
  447.8 19.4 %all-to-all-done.1 = bf16[16,22,1024]{2,1,0:T(8,128)(2,1)S(1)} async-done(((bf16[16,22,1024]{2,1,0:T(8,128)(2,1)}), bf16[16,22,1024]{2,1,0:T(8,128)(2,1)S(1)}, u32[]{:S(2)}, u32[]{:S(2)}) %all-to-all-start.1) | async-done | bytes 720928 | tf_op jit(solution)/shard_map/all_to_all | solution.py:99
  (122 shorter events, 37.6 us)
Async XLA Ops:
  7.2 320.2 %copy-start = (bf16[1,176,1024]{2,1,0:T(8,128)(2,1)S(1)}, bf16[1,176,1024]{2,1,0:T(8,128)(2,1)}, u32[]{:S(2)}) copy-start(bf16[1,176,1024]{2,1,0:T(8,128)(2,1)} %param.18) | copy-start | bytes 1081348
  7.2 92.4 %copy-start.17 = (bf16[88,1024]{1,0:T(8,128)(2,1)S(1)}, bf16[88,1024]{1,0:T(8,128)(2,1)}, u32[]{:S(2)}) copy-start(bf16[88,1024]{1,0:T(8,128)(2,1)} %param.10) | copy-start | bytes 540676
  7.2 93.6 %copy-start.20 = (f32[1024]{0:T(1024)S(1)}, f32[1024]{0:T(1024)}, u32[]{:S(2)}) copy-start(f32[1024]{0:T(1024)} %param.13) | copy-start | bytes 12292
  7.2 92.4 %reduce-scatter.7.cloned.1.call-start = ((), (), s32[]{:S(2)}) async-start(), calls=%async_computation.5 | async-start | bytes 6127616
  11.8 422.2 %reduce-scatter.5.cloned.1.call-start = ((), (), s32[]{:S(2)}) async-start(), calls=%async_computation.4 | async-start | bytes 12255232 | tf_op jit(solution)/shard_map/reduce_scatter | solution.py:92
  134.1 21.5 %collective-permute-start = (bf16[352,1024]{1,0:T(8,128)(2,1)S(1)}, bf16[352,1024]{1,0:T(8,128)(2,1)S(1)}, u32[]{:S(2)}, u32[]{:S(2)}) collective-permute-start(bf16[352,1024]{1,0:T(8,128)(2,1)S(1)} %reshape.166), channel_id=1, source_target_pairs={{0,1},{1,2},{2,3},{3,4},{4,5},{5,6},{6,7},{7,8},{8,9},{9,10},{10,1... | collective-permute-start | bytes 2162696 | tf_op jit(solution)/shard_map/ppermute | solution.py:84
  155.6 20.5 %collective-permute-start.1 = (bf16[352,1024]{1,0:T(8,128)(2,1)S(1)}, bf16[352,1024]{1,0:T(8,128)(2,1)S(1)}, u32[]{:S(2)}, u32[]{:S(2)}) collective-permute-start(bf16[352,1024]{1,0:T(8,128)(2,1)S(1)} %collective-permute-done), channel_id=1, source_target_pairs={{0,1},{1,2},{2,3},{3,4},{4,5},{5,6},{6,7},{7,8},{8,9},{9,10},{10,1... | collective-permute-start | bytes 2162696 | tf_op jit(solution)/shard_map/ppermute | solution.py:84
  155.6 20.5 %collective-permute-start.8 = (bf16[352,1024]{1,0:T(8,128)(2,1)}, bf16[352,1024]{1,0:T(8,128)(2,1)S(1)}, u32[]{:S(2)}, u32[]{:S(2)}) collective-permute-start(bf16[352,1024]{1,0:T(8,128)(2,1)} %copy-done.14), channel_id=1, source_target_pairs={{1,0},{2,1},{3,2},{4,3},{5,4},{6,5},{7,6},{8,7},{9,8},{10,9},{11,1... | collective-permute-start | bytes 2162696 | tf_op jit(solution)/shard_map/ppermute | solution.py:86
  176.1 19.7 %collective-permute-start.2 = (bf16[352,1024]{1,0:T(8,128)(2,1)S(1)}, bf16[352,1024]{1,0:T(8,128)(2,1)S(1)}, u32[]{:S(2)}, u32[]{:S(2)}) collective-permute-start(bf16[352,1024]{1,0:T(8,128)(2,1)S(1)} %collective-permute-done.1), channel_id=1, source_target_pairs={{0,1},{1,2},{2,3},{3,4},{4,5},{5,6},{6,7},{7,8},{8,9},{9,10},{10,1... | collective-permute-start | bytes 2162696 | tf_op jit(solution)/shard_map/ppermute | solution.py:84
  176.1 90.0 %copy-start.1 = (bf16[352,1024]{1,0:T(8,128)(2,1)}, bf16[352,1024]{1,0:T(8,128)(2,1)S(1)}, u32[]{:S(2)}) copy-start(bf16[352,1024]{1,0:T(8,128)(2,1)S(1)} %collective-permute-done.8) | copy-start | bytes 2162692
  176.2 19.7 %collective-permute-start.9 = (bf16[352,1024]{1,0:T(8,128)(2,1)S(1)}, bf16[352,1024]{1,0:T(8,128)(2,1)S(1)}, u32[]{:S(2)}, u32[]{:S(2)}) collective-permute-start(bf16[352,1024]{1,0:T(8,128)(2,1)S(1)} %collective-permute-done.8), channel_id=1, source_target_pairs={{1,0},{2,1},{3,2},{4,3},{5,4},{6,5},{7,6},{8,7},{9,8},{10,9},{11,1... | collective-permute-start | bytes 2162696 | tf_op jit(solution)/shard_map/ppermute | solution.py:86
  195.8 18.8 %collective-permute-start.3 = (bf16[352,1024]{1,0:T(8,128)(2,1)S(1)}, bf16[352,1024]{1,0:T(8,128)(2,1)S(1)}, u32[]{:S(2)}, u32[]{:S(2)}) collective-permute-start(bf16[352,1024]{1,0:T(8,128)(2,1)S(1)} %collective-permute-done.2), channel_id=1, source_target_pairs={{0,1},{1,2},{2,3},{3,4},{4,5},{5,6},{6,7},{7,8},{8,9},{9,10},{10,1... | collective-permute-start | bytes 2162696 | tf_op jit(solution)/shard_map/ppermute | solution.py:84
  195.8 18.8 %collective-permute-start.10 = (bf16[352,1024]{1,0:T(8,128)(2,1)S(1)}, bf16[352,1024]{1,0:T(8,128)(2,1)S(1)}, u32[]{:S(2)}, u32[]{:S(2)}) collective-permute-start(bf16[352,1024]{1,0:T(8,128)(2,1)S(1)} %collective-permute-done.9), channel_id=1, source_target_pairs={{1,0},{2,1},{3,2},{4,3},{5,4},{6,5},{7,6},{8,7},{9,8},{10,9},{11,1... | collective-permute-start | bytes 2162696 | tf_op jit(solution)/shard_map/ppermute | solution.py:86
  214.6 35.1 %copy-start.11 = (bf16[352,1024]{1,0:T(8,128)(2,1)}, bf16[352,1024]{1,0:T(8,128)(2,1)S(1)}, u32[]{:S(2)}) copy-start(bf16[352,1024]{1,0:T(8,128)(2,1)S(1)} %collective-permute-done.3) | copy-start | bytes 2162692
  214.6 18.0 %collective-permute-start.4 = (bf16[352,1024]{1,0:T(8,128)(2,1)S(1)}, bf16[352,1024]{1,0:T(8,128)(2,1)S(1)}, u32[]{:S(2)}, u32[]{:S(2)}) collective-permute-start(bf16[352,1024]{1,0:T(8,128)(2,1)S(1)} %collective-permute-done.3), channel_id=1, source_target_pairs={{0,1},{1,2},{2,3},{3,4},{4,5},{5,6},{6,7},{7,8},{8,9},{9,10},{10,1... | collective-permute-start | bytes 2162696 | tf_op jit(solution)/shard_map/ppermute | solution.py:84
  214.7 17.9 %collective-permute-start.11 = (bf16[352,1024]{1,0:T(8,128)(2,1)S(1)}, bf16[352,1024]{1,0:T(8,128)(2,1)S(1)}, u32[]{:S(2)}, u32[]{:S(2)}) collective-permute-start(bf16[352,1024]{1,0:T(8,128)(2,1)S(1)} %collective-permute-done.10), channel_id=1, source_target_pairs={{1,0},{2,1},{3,2},{4,3},{5,4},{6,5},{7,6},{8,7},{9,8},{10,9},{11,1... | collective-permute-start | bytes 2162696 | tf_op jit(solution)/shard_map/ppermute | solution.py:86
  232.6 17.1 %collective-permute-start.5 = (bf16[352,1024]{1,0:T(8,128)(2,1)S(1)}, bf16[352,1024]{1,0:T(8,128)(2,1)S(1)}, u32[]{:S(2)}, u32[]{:S(2)}) collective-permute-start(bf16[352,1024]{1,0:T(8,128)(2,1)S(1)} %collective-permute-done.4), channel_id=1, source_target_pairs={{0,1},{1,2},{2,3},{3,4},{4,5},{5,6},{6,7},{7,8},{8,9},{9,10},{10,1... | collective-permute-start | bytes 2162696 | tf_op jit(solution)/shard_map/ppermute | solution.py:84
  233.6 16.2 %collective-permute-start.12 = (bf16[352,1024]{1,0:T(8,128)(2,1)S(1)}, bf16[352,1024]{1,0:T(8,128)(2,1)}, u32[]{:S(2)}, u32[]{:S(2)}) collective-permute-start(bf16[352,1024]{1,0:T(8,128)(2,1)S(1)} %collective-permute-done.11), channel_id=1, source_target_pairs={{1,0},{2,1},{3,2},{4,3},{5,4},{6,5},{7,6},{8,7},{9,8},{10,9},{11,1... | collective-permute-start | bytes 2162696 | tf_op jit(solution)/shard_map/ppermute | solution.py:86
  249.7 16.4 %collective-permute-start.6 = (bf16[352,1024]{1,0:T(8,128)(2,1)S(1)}, bf16[352,1024]{1,0:T(8,128)(2,1)}, u32[]{:S(2)}, u32[]{:S(2)}) collective-permute-start(bf16[352,1024]{1,0:T(8,128)(2,1)S(1)} %collective-permute-done.5), channel_id=1, source_target_pairs={{0,1},{1,2},{2,3},{3,4},{4,5},{5,6},{6,7},{7,8},{8,9},{9,10},{10,1... | collective-permute-start | bytes 2162696 | tf_op jit(solution)/shard_map/ppermute | solution.py:84
  249.7 16.6 %collective-permute-start.13 = (bf16[352,1024]{1,0:T(8,128)(2,1)}, bf16[352,1024]{1,0:T(8,128)(2,1)}, u32[]{:S(2)}, u32[]{:S(2)}) collective-permute-start(bf16[352,1024]{1,0:T(8,128)(2,1)} %collective-permute-done.12), channel_id=1, source_target_pairs={{1,0},{2,1},{3,2},{4,3},{5,4},{6,5},{7,6},{8,7},{9,8},{10,9},{11,1... | collective-permute-start | bytes 2162696 | tf_op jit(solution)/shard_map/ppermute | solution.py:86
  266.1 15.7 %collective-permute-start.7 = (bf16[352,1024]{1,0:T(8,128)(2,1)}, bf16[352,1024]{1,0:T(8,128)(2,1)}, u32[]{:S(2)}, u32[]{:S(2)}) collective-permute-start(bf16[352,1024]{1,0:T(8,128)(2,1)} %collective-permute-done.6), channel_id=1, source_target_pairs={{0,1},{1,2},{2,3},{3,4},{4,5},{5,6},{6,7},{7,8},{8,9},{9,10},{10,1... | collective-permute-start | bytes 2162696 | tf_op jit(solution)/shard_map/ppermute | solution.py:84
  266.4 39.4 %collective-permute-start.14 = (bf16[352,1024]{1,0:T(8,128)(2,1)}, bf16[352,1024]{1,0:T(8,128)(2,1)S(1)}, u32[]{:S(2)}, u32[]{:S(2)}) collective-permute-start(bf16[352,1024]{1,0:T(8,128)(2,1)} %collective-permute-done.13), channel_id=1, source_target_pairs={{1,0},{2,1},{3,2},{4,3},{5,4},{6,5},{7,6},{8,7},{9,8},{10,9},{11,1... | collective-permute-start | bytes 2162696 | tf_op jit(solution)/shard_map/ppermute | solution.py:86
  340.5 104.4 %copy-start.18 = (f32[1024,16]{0,1:T(8,128)S(1)}, f32[1024,16]{0,1:T(8,128)}, u32[]{:S(2)}) copy-start(f32[1024,16]{0,1:T(8,128)} %param.14) | copy-start | bytes 196612
  436.1 31.1 %all-to-all-start.1 = ((bf16[16,22,1024]{2,1,0:T(8,128)(2,1)}), bf16[16,22,1024]{2,1,0:T(8,128)(2,1)S(1)}, u32[]{:S(2)}, u32[]{:S(2)}) async-start(bf16[16,22,1024]{2,1,0:T(8,128)(2,1)} %reshape.168), calls=%async_computation.2 | async-start | bytes 1572864 | tf_op jit(solution)/shard_map/all_to_all | solution.py:99
  (17 other events, 290.1 us)
Sparse Core Ops, SparseCore 0:
  11.9 87.6 reduce-scatter.6
  340.6 93.2 reduce-scatter.4
